TPU v7x, 128 devices: a whole 4x4x4 slice. The times are simulated.
128 devices in a mesh: seq: 32 (over x, z, core), tp: 4 (over y).
Axes of the slice: x: 4, y: 4, z: 4, core: 2. Of those that a mesh axis runs over, the one named last changes fastest.
Arguments:
- tokens: bfloat16 [8192, 2048], P('seq'), may hold values from -6 to 6
- norm_gain: float32 [2048], replicated, may hold values from 0.1 to 1.9
- qkv_weight: bfloat16 [2048, 4096], P(None, 'tp'), may hold values from -0.125 to 0.125
- conv_weight: float32 [4, 4096], P(None, 'tp'), may hold values from -3 to 3
- gate_down: bfloat16 [2048, 16], replicated, may hold values from -0.125 to 0.125
- gate_up: bfloat16 [16, 1024], P(None, 'tp'), may hold values from -6 to 6
- gate_bias: float32 [1024], P('tp'), may hold values from 0.3 to 8.5
- out_gate_weight: bfloat16 [2048, 2048], P(None, 'tp'), may hold values from -0.125 to 0.125
- head_gain: float32 [512], replicated, may hold values from 0.1 to 1.9
- out_weight: bfloat16 [2048, 2048], P('tp'), may hold values from -0.125 to 0.125
- final_gain: float32 [2048], replicated, may hold values from 0.1 to 1.9
- embedding: bfloat16 [32000, 2048], P(('seq', 'tp')), may hold values from -0.5 to 0.5
- lengths: int32 [8], replicated, may hold values from 1 to 4096, as said below
- packed_order: int32 [8], replicated, may hold values from 0 to 7, each once
Outputs:
- hidden: bfloat16 [8192, 2048], P('seq', 'tp')
- last_states: float32 [8, 4, 256, 512], P(None, 'tp')
- conv_edges: float32 [8, 3, 4096], P(None, None, 'tp')
- last_norms: float32 [8], replicated
- max_logits: float32 [8, 128], P(None, ('seq', 'tp'))
Inputs may be any that keep to these rules, and one draw needn't show every extreme that they name: Request r of the initial order has lengths[r] tokens; the lengths sum to 8192, the largest is 4096 and the smallest is 1 or 2. packed_order names every request once; the packed positions hold the tokens of request packed_order[0], then those of packed_order[1], and so on.
All inputs are finite; a program needn't handle non-finite values.
Results may differ from a plain program's by a relative error of at most 0.015.
Values may be sent and summed in bfloat16 or wider, within the bound.
No kernel may reach another device: no remote copies, remote signals or barrier semaphores. Data moves between devices by JAX's collectives and lax.ppermute only.
A program may use at most 128 MiB of HBM per device.

v0:
```python
from functools import partial
import jax
import jax.numpy as jnp
from jax import lax
from jax.sharding import PartitionSpec as P

DK = 256
DV = 512
KCONV = 4
BLOCK = 64
HIGHEST_PRECISION = lax.Precision.HIGHEST


def prefix(array, axis, combine, identity):
    peers, place = (lax.axis_size(axis), lax.axis_index(axis))
    everything = jax.tree.map(
        lambda part, kind: lax.all_gather(part.astype(kind), axis),
        array,
        (jnp.bfloat16, jnp.bfloat16),
    )
    start = jax.tree.map(
        lambda part, zero: jnp.broadcast_to(jnp.asarray(zero, part.dtype), part.shape),
        array,
        identity,
    )

    def hop(k, before):
        reached = k < place
        new = combine(
            before, jax.tree.map(lambda part, own: part[k].astype(own.dtype), everything, array)
        )
        return jax.tree.map(lambda a, b: jnp.where(reached, a, b), new, before)

    return lax.fori_loop(0, peers, hop, start)


def passed_along(array, axis, by):
    peers = lax.axis_size(axis)
    pairs = [(i, i + by) for i in range(peers) if 0 <= i + by < peers]
    return lax.ppermute(array, axis, pairs)


def segments(lengths, packed_order, positions):
    request_count = lengths.shape[0]
    select = (packed_order[:, None] == jnp.arange(request_count, dtype=jnp.int32)[None, :]).astype(
        jnp.int32
    )
    packed_len = jnp.sum(select * lengths[None, :], axis=1)
    end_points = jnp.cumsum(packed_len)
    starts = end_points - packed_len
    segment = jnp.sum((positions[:, None] >= starts[None, :]).astype(jnp.int32), axis=1) - 1
    last_index = jnp.sum(select * (end_points - 1)[:, None], axis=0)
    return (segment, last_index)


def causal_conv(padded, padded_segment, conv_weight, row_count):
    running = jnp.zeros((row_count, padded.shape[1]), jnp.float32)
    current = padded_segment[KCONV - 1 :]
    for offset in range(KCONV):
        window = padded[offset : offset + row_count]
        same_segment = (padded_segment[offset : offset + row_count] == current)[:, None]
        running = running + jnp.where(same_segment, window, 0.0) * conv_weight[offset]
    return running


def activate(convolved, head_count):
    shaped = convolved.reshape(convolved.shape[0], head_count, 2 * DK + DV)
    channel = jnp.arange(2 * DK + DV)
    return jnp.where(channel < 2 * DK, jax.nn.silu(shaped), shaped).astype(jnp.bfloat16)


def advance(carry_state, key_floats, values, cumulative, segment, segment_before):
    total_decay = cumulative[-1]
    same_tail = (segment == segment[-1])[:, None, None]
    scaled = jnp.where(same_tail, key_floats * jnp.exp(total_decay[None] - cumulative), 0.0).astype(
        jnp.bfloat16
    )
    added = jnp.einsum("jhc,jhv->hcv", scaled, values, preferred_element_type=jnp.float32)
    through = segment[-1] == segment_before
    return jnp.where(through, jnp.exp(total_decay)[:, :, None] * carry_state, 0.0) + added


def state_at_ends(
    end_states, carry_state, key_floats, values, cumulative, segment, segment_before, offset
):
    length = segment.shape[0]
    inside_block = (offset >= 0) & (offset < length)

    def add_ends(previous):
        end_row = jnp.clip(offset, 0, length - 1)
        end_decay = cumulative[end_row]
        end_segment = segment[end_row]
        indices = jnp.arange(length)
        allowed = (
            (indices[None, :] <= end_row[:, None]) & (segment[None, :] == end_segment[:, None])
        )[:, :, None, None]
        spread = jnp.where(allowed, end_decay[:, None] - cumulative[None], 0.0)
        weighted = jnp.where(allowed, key_floats[None] * jnp.exp(spread), 0.0).astype(jnp.bfloat16)
        within = jnp.einsum("rjhc,jhv->rhcv", weighted, values, preferred_element_type=jnp.float32)
        carried = (end_segment == segment_before)[:, None, None, None]
        reached = jnp.where(carried, jnp.exp(end_decay)[:, :, :, None] * carry_state[None], 0.0)
        return jnp.where(inside_block[:, None, None, None], within + reached, previous)

    def keep(previous):
        return previous

    return lax.cond(jnp.any(inside_block), add_ends, keep, end_states)


def block_step(last_index, carry, inputs):
    carry_state, end_states = carry
    queries, key_rows, values, decays, segment, segment_before, block_first = inputs
    cumulative = jnp.cumsum(decays, axis=0)
    length = segment.shape[0]
    indices = jnp.arange(length)
    causal = (indices[None, :] <= indices[:, None]) & (segment[None, :] == segment[:, None])
    allowed = causal[:, :, None, None]
    spread = jnp.where(allowed, cumulative[:, None] - cumulative[None, :], 0.0)
    weights = jnp.where(allowed, jnp.exp(spread), 0.0)
    query_rows = queries.astype(jnp.float32)
    key_floats = key_rows.astype(jnp.float32)
    scores = jnp.sum(query_rows[:, None] * key_floats[None, :] * weights, axis=-1).astype(
        jnp.bfloat16
    )
    inside = jnp.einsum("ijh,jhv->ihv", scores, values, preferred_element_type=jnp.float32)
    carried = (segment == segment_before)[:, None, None]
    outside = jnp.einsum(
        "ihc,hcv->ihv", query_rows * jnp.exp(cumulative), carry_state, precision=HIGHEST_PRECISION
    )
    output = inside + jnp.where(carried, outside, 0.0)
    new_state = advance(carry_state, key_floats, values, cumulative, segment, segment_before)
    end_states = state_at_ends(
        end_states,
        carry_state,
        key_floats,
        values,
        cumulative,
        segment,
        segment_before,
        last_index - block_first,
    )
    return ((new_state, end_states), output)


def state_only(carry_state, inputs):
    block_queries, block_keys, block_values, block_decays, block_segment, before, block_start = (
        inputs
    )
    cumulative = jnp.cumsum(block_decays, axis=0)
    return (
        advance(
            carry_state,
            block_keys.astype(jnp.float32),
            block_values,
            cumulative,
            block_segment,
            before,
        ),
        None,
    )


def head_output(attended, gate_out, head_gain):
    row_count, head_count, value_width = attended.shape
    mean_square = jnp.mean(attended * attended, axis=2, keepdims=True)
    gate_values = jax.nn.silu(
        gate_out.astype(jnp.float32).reshape(row_count, head_count, value_width)
    )
    gated = attended * lax.rsqrt(mean_square + 1e-05) * head_gain * gate_values
    return gated.reshape(row_count, head_count * value_width).astype(jnp.bfloat16)


def carry_in(decay_factor, local_state):

    def combine(earlier, later):
        return (earlier[0] * later[0], later[0][:, :, None] * earlier[1] + later[1])

    identity = (jnp.ones_like(decay_factor), jnp.zeros_like(local_state))
    result = prefix((decay_factor, local_state), "seq", combine, identity)
    return result[1]


def shards(
    tokens,
    norm_gain,
    qkv_weight,
    conv_weight,
    gate_down,
    gate_up,
    gate_bias,
    out_gate_weight,
    head_gain,
    out_weight,
    final_gain,
    embedding,
    lengths,
    packed_order,
):
    row_count = tokens.shape[0]
    head_count = out_weight.shape[0] // DV
    column_count = tokens.shape[1] // lax.axis_size("tp")
    start_row = lax.axis_index("seq") * row_count
    positions = start_row + jnp.arange(-(KCONV - 1), row_count, dtype=jnp.int32)
    segment_all, last_index = segments(lengths, packed_order, positions)
    segment = segment_all[KCONV - 1 :]
    segment_prior = segment_all[KCONV - 2]
    first_index = last_index - lengths + 1
    residual = tokens.astype(jnp.float32)
    normed = (
        residual
        * lax.rsqrt(jnp.mean(residual * residual, axis=1, keepdims=True) + 1e-06)
        * norm_gain
    ).astype(jnp.bfloat16)
    projected = jnp.dot(normed, qkv_weight, preferred_element_type=jnp.float32).astype(jnp.bfloat16)
    rim_rows = passed_along(projected[row_count - (KCONV - 1) :], "seq", 1)
    padded = jnp.concatenate([rim_rows, projected], axis=0)
    convolved = causal_conv(padded.astype(jnp.float32), segment_all, conv_weight, row_count)
    activated = activate(convolved, head_count)
    queries = activated[:, :, :DK]
    key_rows = activated[:, :, DK : 2 * DK]
    values = activated[:, :, 2 * DK :]
    lowrank = jnp.dot(normed, gate_down, preferred_element_type=jnp.float32)
    gate_logits = (
        jnp.dot(lowrank, gate_up.astype(jnp.float32), precision=HIGHEST_PRECISION) + gate_bias
    )
    decays = (jax.nn.log_sigmoid(gate_logits) / 16.0).reshape(row_count, head_count, DK)
    gate_out = jnp.dot(normed, out_gate_weight, preferred_element_type=jnp.float32).astype(
        jnp.bfloat16
    )
    block_count = row_count // BLOCK

    def split_blocks(array):
        return array.reshape((block_count, BLOCK) + array.shape[1:])

    segment_before = segment_all[KCONV - 2 : KCONV - 2 + row_count : BLOCK]
    block_first = start_row + jnp.arange(block_count, dtype=jnp.int32) * BLOCK
    block_inputs = (
        split_blocks(queries),
        split_blocks(key_rows),
        split_blocks(values),
        split_blocks(decays),
        split_blocks(segment),
        segment_before,
        block_first,
    )
    through_shard = segment[-1] == segment_prior
    empty_state = jnp.zeros((head_count, DK, DV), jnp.float32)
    empty_ends = jnp.zeros((lengths.shape[0], head_count, DK, DV), jnp.float32)
    stepper = partial(block_step, last_index)
    local_state, unused_steps = lax.scan(state_only, empty_state, block_inputs)
    decay_factor = jnp.where(through_shard, jnp.exp(jnp.sum(decays, axis=0)), 0.0)
    incoming = carry_in(decay_factor, local_state)
    (unused_state, end_states), attended = lax.scan(stepper, (incoming, empty_ends), block_inputs)
    attended = attended.reshape(row_count, head_count, DV)
    gated = head_output(attended, gate_out, head_gain)
    projected_out = jnp.dot(gated, out_weight, preferred_element_type=jnp.float32)
    summed = lax.psum_scatter(
        projected_out.astype(jnp.bfloat16), "tp", scatter_dimension=1, tiled=True
    ).astype(jnp.float32)
    column_start = lax.axis_index("tp") * column_count
    own_columns = lax.dynamic_slice_in_dim(residual, column_start, column_count, 1)
    hidden = (own_columns + summed).astype(jnp.bfloat16)
    owned_here = (last_index >= start_row) & (last_index < start_row + row_count)
    local_last = jnp.clip(last_index - start_row, 0, row_count - 1)
    last_rows = jnp.where(owned_here[:, None], hidden[local_last].astype(jnp.float32), 0.0)
    edge_list = []
    for offset in range(KCONV - 1):
        located = last_index - (KCONV - 2) + offset
        inside = owned_here & (located >= first_index)
        picked = padded[jnp.clip(located - start_row + KCONV - 1, 0, row_count + KCONV - 2)].astype(
            jnp.float32
        )
        edge_list.append(jnp.where(inside[:, None], picked, 0.0))
    conv_edges = jnp.stack(edge_list, axis=1)
    row_sums, conv_edges, last_states = (
        lax.psum(last_rows.astype(jnp.bfloat16), "seq").astype(jnp.float32),
        lax.psum(conv_edges.astype(jnp.bfloat16), "seq").astype(jnp.float32),
        lax.psum(end_states.astype(jnp.bfloat16), "seq").astype(jnp.float32),
    )
    full_rows = lax.all_gather(row_sums, "tp", axis=1, tiled=True)
    mean_square = jnp.mean(full_rows * full_rows, axis=1)
    last_norms = jnp.sqrt(mean_square)
    final_rows = (full_rows * lax.rsqrt(mean_square[:, None] + 1e-06) * final_gain).astype(
        jnp.bfloat16
    )
    logits = jnp.dot(final_rows, embedding.T, preferred_element_type=jnp.float32)
    max_logits = jnp.max(logits, axis=1, keepdims=True)
    return (hidden, last_states, conv_edges, last_norms, max_logits)


def solution(mesh):
    in_specs = (
        P("seq", None),
        P(),
        P(None, "tp"),
        P(None, "tp"),
        P(),
        P(None, "tp"),
        P("tp"),
        P(None, "tp"),
        P(),
        P("tp", None),
        P(),
        P(("seq", "tp"), None),
        P(),
        P(),
    )
    out_specs = (
        P("seq", "tp"),
        P(None, "tp", None, None),
        P(None, None, "tp"),
        P(),
        P(None, ("seq", "tp")),
    )
    return jax.shard_map(shards, mesh=mesh, in_specs=in_specs, out_specs=out_specs, check_vma=False)
```

profile of v0, /device:TPU:0, one launch (start us, length us, event | category | flops | bytes accessed | tf_op | source)
XLA Modules:
  0.0 477.1 jit_solution(16728195551736005816)
XLA Ops:
  7.2 1.6 multiply_reduce_fusion.1
  9.0 3.9 convolution_convert_fusion.1
  12.9 1.3 collective-permute-start
  14.8 1.7 fusion.70
  17.2 1.0 copy.52
  18.2 1.0 pad_maximum_fusion
  21.1 21.8 %while.43 = (s32[]{:T(128)}, f32[1,256,512]{2,1,0:T(8,128)S(1)}, s32[4,64]{1,0:T(4,128)S(1)}, s32[4]{0:T(128)S(1)}, f32[4,64,1,256]{3,2,1,0:T(1,128)}, /*index=5...) while((s32[]{:T(128)}, f32[1,256,512]{2,1,0:T(8,128)S(1)}, ...), condition=%wide.region_7.8_spmd.clone, body=%wide.region_5.7_spmd.clone.sunk | while | flops 18415684 | bytes 1417237 | solution.py:250
  25.3 1.2 fusion.123
  30.8 1.2 fusion.123
  36.2 1.2 fusion.123
  41.7 1.2 fusion.123
  45.5 26.3 %all-gather.2 = bf16[32,1,256]{2,1,0:T(2,128)(2,1)S(1)} all-gather(bf16[1,1,256]{2,1,0:T(2,128)(2,1)S(1)} %reshape.975), channel_id=2, replica_groups=mesh['seq'=32,'tp'=4] {'seq'}, dimensions={0}, use_global_device_ids=true | all-gather | bytes 16896 | tf_op jit(solution)/shard_map/all_gather | solution.py:17
  71.9 29.0 %all-gather.5.cloned.1.call-done = bf16[32,256,512]{2,1,0:T(8,128)(2,1)} async-done(((bf16[1,256,512]{2,1,0:T(8,128)(2,1)}), bf16[32,256,512]{2,1,0:T(8,128)(2,1)}) %all-gather.5.cloned.1.call-update) | async-done | bytes 8388624 | tf_op jit(solution)/shard_map/all_gather | solution.py:17
  101.0 36.2 %while.44 = (s32[]{:T(128)}, f32[1,256,512]{2,1,0:T(8,128)S(1)}, s32[]{:T(128)}, bf16[32,1,256]{2,1,0:T(2,128)(2,1)S(1)}, bf16[32,1,256,512]{3,2,1,0:T(8,128)(2,1)}, /*index=5*/s32[]{:T(128)}, s32[]{:T(128)}) while((s32[]{:T(128)}, f32[1,256,512]{2,1,0:T(8,128)S(1)}, s32[]{:T(128)}, bf16[32,1,256]{2,1,0:T(2,128)(2,1)S(1)}, ...), condition=%wide.region_9.10_spmd.clone, body=%wide.region_8.9_spmd.clone.sunk | while | flops 655620 | bytes 1313385 | solution.py:34
  101.0 1.1 fusion.124
  102.1 1.1 fusion.124
  103.2 1.1 fusion.124
  104.4 1.1 fusion.124
  105.5 1.1 fusion.124
  106.6 1.1 fusion.124
  107.7 1.1 fusion.124
  108.9 1.1 fusion.124
  110.0 1.1 fusion.124
  111.1 1.1 fusion.124
  112.3 1.1 fusion.124
  113.4 1.1 fusion.124
  114.5 1.1 fusion.124
  115.7 1.1 fusion.124
  116.8 1.1 fusion.124
  117.9 1.1 fusion.124
  119.1 1.1 fusion.124
  120.2 1.1 fusion.124
  121.3 1.1 fusion.124
  122.5 1.1 fusion.124
  123.6 1.1 fusion.124
  124.7 1.1 fusion.124
  125.9 1.1 fusion.124
  127.0 1.1 fusion.124
  128.1 1.1 fusion.124
  129.2 1.1 fusion.124
  130.4 1.1 fusion.124
  131.5 1.1 fusion.124
  132.6 1.1 fusion.124
  133.8 1.1 fusion.124
  134.9 1.1 fusion.124
  136.0 1.1 fusion.124
  137.1 1.5 broadcast_in_dim.240
  138.6 54.6 %while.42 = (s32[]{:T(128)}, f32[1,256,512]{2,1,0:T(8,128)S(1)}, bf16[8,1,256,512]{3,2,0,1:T(8,128)(2,1)}, f32[4,64,1,512]{3,1,2,0:T(8,128)}, s32[4,64]{1,0:T(4,...) while((s32[]{:T(128)}, f32[1,256,512]{2,1,0:T(8,128)S(1)}, ...), condition=%wide.region_17.18_spmd, body=%wide.region_11.17_spmd.sunk | while | flops 268659424 | bytes 8804605 | solution.py:253
  144.4 5.7 %conditional.2 = (bf16[8,1,256,512]{3,2,0,1:T(8,128)(2,1)}) conditional(s32[]{:T(128)} %convert_element_type.388, bf16[8,1,256,512]{3,2,0,1:T(8,128)(2,1)} %get-tuple-element.722, (pred[8]{0:T(512)(128)(4,1)S(1)}, s32[8]{0:T(128)S(1)}, s32[64]{0:T(128)S(1)}, bf16[1,64,1,256]{3,2,1,0:T(2,128)(2,1)S(1)}, f32[64,1,256]{2,1,0:T(1,128)S(1)}, ...), branch_computations={%region_14.14_spmd, %region_15.15_spmd} | conditional | flops 139086368 | bytes 5199492 | solution.py:107
  146.4 3.7 fusion
  150.3 2.0 multiply_reduce_fusion.5
  162.5 2.0 multiply_reduce_fusion.5
  174.7 2.0 multiply_reduce_fusion.5
  187.0 2.0 multiply_reduce_fusion.5
  194.5 2.8 fusion.56
  197.3 1.7 convolution_convert_fusion
  199.0 2.8 convert_element_type.287
  203.9 96.7 %all-reduce.3.cloned.1.call-done = bf16[8,1,256,512]{3,2,1,0:T(8,128)(2,1)} async-done(((bf16[8,1,256,512]{3,2,1,0:T(8,128)(2,1)}), bf16[8,1,256,512]{3,2,1,0:T(8,128)(2,1)}) %all-reduce.3.cloned.1.call-update) | async-done | bytes 2097168 | tf_op jit(solution)/shard_map/psum | solution.py:278
  300.6 4.2 convert_element_type.304
  304.8 21.7 %reduce-scatter.2.cloned.1.call-done = bf16[256,512]{1,0:T(8,128)(2,1)} async-done(((bf16[256,2048]{1,0:T(8,128)(2,1)}), bf16[256,512]{1,0:T(8,128)(2,1)}) %reduce-scatter.2.cloned.1.call-update) | async-done | bytes 262160 | tf_op jit(solution)/shard_map/reduce_scatter | solution.py:257
  326.5 1.2 add_convert_fusion
  328.3 126.8 %all-reduce = (bf16[8,3,1024]{2,0,1:T(8,128)(2,1)S(1)}, bf16[8,512]{1,0:T(8,128)(2,1)S(1)}) all-reduce(bf16[8,3,1024]{2,0,1:T(8,128)(2,1)S(1)} %pad_maximum_fusion.1, bf16[8,512]{1,0:T(8,128)(2,1)S(1)} %select_convert_fusion.2), channel_id=1, replica_groups=mesh['seq'=32,'tp'=4] {'seq'}, use_global_device_ids=true, to_apply=%region_21.22 | all-reduce | flops 28672 | bytes 114688 | tf_op jit(solution)/shard_map/psum | solution.py:277
  455.2 11.9 %all_gather.16 = f32[8,2048]{1,0:T(8,128)S(1)} all-gather(f32[8,512]{1,0:T(8,128)S(1)} %convert_element_type.314), channel_id=1, replica_groups=mesh['seq'=32,'tp'=4] {'tp'}, dimensions={1}, use_global_device_ids=true | all-gather | bytes 81920 | tf_op jit(solution)/shard_map/all_gather | solution.py:280
  468.3 2.2 convolution_reduce_fusion
  (243 shorter events, 56.2 us)
Async XLA Ops:
  7.2 190.1 %copy-start = (bf16[512,2048]{1,0:T(8,128)(2,1)S(1)}, bf16[512,2048]{1,0:T(8,128)(2,1)}, u32[]{:S(2)}) copy-start(bf16[512,2048]{1,0:T(8,128)(2,1)} %param.31) | copy-start | bytes 6291460
  7.2 93.8 %all-gather.5.cloned.1.call-start = ((), (), s32[]{:S(2)}) async-start(), calls=%async_computation.3 | async-start | bytes 8650752 | tf_op jit(solution)/shard_map/all_gather | solution.py:17
  8.9 5.3 %copy-start.6 = (s32[8]{0:T(128)S(1)}, s32[8]{0:T(128)}, u32[]{:S(2)}) copy-start(s32[8]{0:T(128)} %param.34) | copy-start | bytes 100
  8.9 5.3 %copy-start.12 = (s32[8]{0:T(128)S(1)}, s32[8]{0:T(128)}, u32[]{:S(2)}) copy-start(s32[8]{0:T(128)} %param.35) | copy-start | bytes 100
  8.9 5.8 %copy-start.4 = (f32[4,1024]{1,0:T(4,128)S(1)}, f32[4,1024]{1,0:T(4,128)}, u32[]{:S(2)}) copy-start(f32[4,1024]{1,0:T(4,128)} %param.25) | copy-start | bytes 49156
  8.9 5.8 %copy-start.7 = (bf16[2048,16]{0,1:T(8,128)(2,1)S(1)}, bf16[2048,16]{0,1:T(8,128)(2,1)}, u32[]{:S(2)}) copy-start(bf16[2048,16]{0,1:T(8,128)(2,1)} %param.26) | copy-start | bytes 196612
  8.9 5.8 %copy-start.9 = (f32[2048]{0:T(1024)S(1)}, f32[2048]{0:T(1024)}, u32[]{:S(2)}) copy-start(f32[2048]{0:T(1024)} %param.23) | copy-start | bytes 24580
  8.9 7.5 %copy-start.8 = (bf16[16,256]{1,0:T(8,128)(2,1)S(1)}, bf16[16,256]{1,0:T(8,128)(2,1)}, u32[]{:S(2)}) copy-start(bf16[16,256]{1,0:T(8,128)(2,1)} %param.27) | copy-start | bytes 24580
  9.0 7.5 %copy-start.11 = (f32[256]{0:T(256)S(1)}, f32[256]{0:T(256)}, u32[]{:S(2)}) copy-start(f32[256]{0:T(256)} %param.28) | copy-start | bytes 3076
  12.9 5.3 %collective-permute-start = (bf16[3,1024]{1,0:T(4,128)(2,1)S(1)}, bf16[3,1024]{1,0:T(4,128)(2,1)S(1)}, u32[]{:S(2)}, u32[]{:S(2)}) collective-permute-start(bf16[3,1024]{1,0:T(4,128)(2,1)S(1)} %slice.111), channel_id=1, source_target_pairs={{0,4},{4,8},{8,12},{12,16},{16,20},{20,24},{24,28},{28,32},{32,36}... | collective-permute-start | bytes 18440 | tf_op jit(solution)/shard_map/ppermute | solution.py:40
  43.6 257.0 %all-reduce.3.cloned.1.call-start = ((), (), s32[]{:S(2)}) async-start(), calls=%async_computation.2 | async-start | bytes 4194304 | tf_op jit(solution)/shard_map/psum | solution.py:278
  193.3 1.0 copy-start.2
  193.3 1.2 copy-start.10
  193.3 133.2 %reduce-scatter.2.cloned.1.call-start = ((), (), s32[]{:S(2)}) async-start(), calls=%async_computation.1 | async-start | bytes 1310720 | tf_op jit(solution)/shard_map/reduce_scatter | solution.py:257
  199.0 2.9 copy-start.1
  203.9 264.4 %copy-start.5 = (f32[2048]{0:T(1024)S(1)}, f32[2048]{0:T(1024)}, u32[]{:S(2)}) copy-start(f32[2048]{0:T(1024)} %param.32) | copy-start | bytes 24580
  327.7 142.9 %copy-start.3 = (bf16[256,512]{1,0:T(8,128)(2,1)}, bf16[256,512]{1,0:T(8,128)(2,1)S(1)}, u32[]{:S(2)}) copy-start(bf16[256,512]{1,0:T(8,128)(2,1)S(1)} %add_convert_fusion) | copy-start | bytes 786436
Sparse Core Ops, SparseCore 0:
  43.7 57.1 all-gather.4
  193.4 107.1 all-reduce.2
  303.0 23.4 reduce-scatter.1
where the time goes:
time: 480 us; the launch traced here: 477 us
  blocking collectives  165 us (34%)
  waiting for transfers between devices  147 us (31%)
  other arithmetic  81.7 us (17%)
  matrix products  27.2 us (6%)
  local copies, waits for them, and re-layouts  24.3 us (5%)
  between operations  15.3 us (3%)
  loops' own time  14.8 us (3%)
    psum x1, blocking collectives, shards(): lax.psum(conv_edges.astype(jnp.bfloat16), 'seq').astype(jnp.float32)  127 us
    psum x1, waiting for transfers between devices, shards(): lax.psum(end_states.astype(jnp.bfloat16), 'seq').astype(jnp.float32)  96.7 us
    select_n x32, other arithmetic, hop(): return jax.tree.map(lambda a, b: jnp.where(reached, a, b), new, before)  34.9 us
    all_gather x1, waiting for transfers between devices, prefix(): lax.all_gather(part.astype(kind), axis)  29 us
    all_gather x1, blocking collectives, prefix(): lax.all_gather(part.astype(kind), axis)  26.3 us
    reduce_scatter x1, waiting for transfers between devices, shards(): lax.psum_scatter(projected_out.astype(jnp.bfloat16), 'tp', scatter_dimens...  21.7 us
    all_gather x1, blocking collectives, shards(): full_rows = lax.all_gather(row_sums, 'tp', axis=1, tiled=True)  11.9 us
    dynamic_slice x24, local copies, waits for them, and re-layouts, shards(): local_state, unused_steps = lax.scan(state_only, empty_state, block_inputs)  10.5 us
  transfers between devices with their start and end apart: 4, of which 3 were waited for; matrix products, arithmetic and copies ran while one was open for 4% of the time, Pallas kernels for 0%

commit v1 on v0

--- a/solution.py
+++ b/solution.py
@@ -9,6 +9,13 @@
 KCONV = 4
 BLOCK = 64
 HIGHEST_PRECISION = lax.Precision.HIGHEST
+
+
+def tell_boxes(raw, mesh_name):
+    long_array = lax.axis_size(mesh_name)
+    met_up = jnp.stack([raw] * long_array)
+    back = lax.all_to_all(met_up, mesh_name, 0, 0)
+    return jnp.concatenate(back, axis=1)
 
 
 def prefix(array, axis, combine, identity):
@@ -277,7 +284,7 @@
         lax.psum(conv_edges.astype(jnp.bfloat16), "seq").astype(jnp.float32),
         lax.psum(end_states.astype(jnp.bfloat16), "seq").astype(jnp.float32),
     )
-    full_rows = lax.all_gather(row_sums, "tp", axis=1, tiled=True)
+    full_rows = tell_boxes(row_sums, mesh_name="tp")
     mean_square = jnp.mean(full_rows * full_rows, axis=1)
     last_norms = jnp.sqrt(mean_square)
     final_rows = (full_rows * lax.rsqrt(mean_square[:, None] + 1e-06) * final_gain).astype(

time: 480 us -> 372 us (0.78)
  waiting for transfers between devices: 147 us -> 45.3 us
  blocking collectives: 165 us -> 154 us
    psum x1, waiting for transfers between devices: 96.7 us -> 0.02 us  [shards(): lax.psum(end_states.astype(jnp.bfloat16), 'seq').astype(jnp.float32)]
    all_gather x1 -> x0, blocking collectives: 11.9 us -> none  [shards(): full_rows = lax.all_gather(row_sums, 'tp', axis=1, tiled=True)]
    reduce_scatter x1, waiting for transfers between devices: 21.7 us -> 16.3 us  [shards(): lax.psum_scatter(projected_out.astype(jnp.bfloat16), 'tp', scatter_dimens...]
  transfers between devices with their start and end apart: 4 -> 5, of which waited for: 3 -> 3; matrix products, arithmetic and copies ran while one was open for 4% -> 5% of each run, Pallas kernels for 0% -> 0%
where the time goes in v1:
time: 372 us; the launch traced here: 370 us
  blocking collectives  154 us (41%)
  other arithmetic  82.6 us (22%)
  waiting for transfers between devices  45.3 us (12%)
  local copies, waits for them, and re-layouts  28.1 us (8%)
  matrix products  24.8 us (7%)
  between operations  15.3 us (4%)
  loops' own time  14.8 us (4%)
  starting transfers between devices  4.69 us (1%)
    psum x1, blocking collectives, shards(): lax.psum(conv_edges.astype(jnp.bfloat16), 'seq').astype(jnp.float32)  127 us
    select_n x32, other arithmetic, hop(): return jax.tree.map(lambda a, b: jnp.where(reached, a, b), new, before)  34.9 us
    all_gather x1, waiting for transfers between devices, prefix(): lax.all_gather(part.astype(kind), axis)  28.3 us
    all_gather x1, blocking collectives, prefix(): lax.all_gather(part.astype(kind), axis)  27 us
    reduce_scatter x1, waiting for transfers between devices, shards(): lax.psum_scatter(projected_out.astype(jnp.bfloat16), 'tp', scatter_dimens...  16.3 us
    dynamic_slice x24, local copies, waits for them, and re-layouts, shards(): local_state, unused_steps = lax.scan(state_only, empty_state, block_inputs)  10.5 us
    another operation x1, loops' own time, shards(): lax.scan(stepper, (incoming, empty_ends), block_inputs)  8.29 us
    reduce_sum x4, other arithmetic, block_step(): jnp.sum(query_rows[:, None] * key_floats[None, :] * weights, axis=-1)  8.17 us
  transfers between devices with their start and end apart: 5, of which 3 were waited for; matrix products, arithmetic and copies ran while one was open for 5% of the time, Pallas kernels for 0%

profile of v1, /device:TPU:0, one launch (start us, length us, event | category | flops | bytes accessed | tf_op | source)
XLA Modules:
  0.0 369.8 jit_solution(17331438721502687646)
XLA Ops:
  7.2 1.6 multiply_reduce_fusion.1
  9.0 3.9 %convolution_convert_fusion.1 = bf16[256,1024]{1,0:T(8,128)(2,1)S(1)} fusion(bf16[2048,1024]{1,0:T(8,128)(2,1)} %param.24, f32[2048]{0:T(1024)} %param.23, f32[256]{0:T(256)S(1)} %add_rsqrt_fusion.1, bf16[256,2048]{1,0:T(8,128)(2,1)} %param.22), kind=kOutput, calls=%fused_computation.94 | convolution fusion | flops 1076101120 | bytes 5776384 | tf_op jit(solution)/shard_map/dot_general | solution.py:221
  13.7 1.3 collective-permute-start
  17.8 2.1 pad_maximum_fusion
  21.7 21.8 %while.43 = (s32[]{:T(128)}, f32[1,256,512]{2,1,0:T(8,128)S(1)}, s32[4,64]{1,0:T(4,128)S(1)}, s32[4]{0:T(128)S(1)}, f32[4,64,1,256]{3,2,1,0:T(1,128)}, /*index=5...) while((s32[]{:T(128)}, f32[1,256,512]{2,1,0:T(8,128)S(1)}, ...), condition=%wide.region_7.8_spmd.clone, body=%wide.region_5.7_spmd.clone.sunk | while | flops 18415684 | bytes 1417237 | solution.py:257
  26.0 1.2 fusion.124
  31.4 1.2 fusion.124
  36.9 1.2 fusion.124
  42.3 1.2 fusion.124
  46.2 27.0 %all-gather.2 = bf16[32,1,256]{2,1,0:T(2,128)(2,1)S(1)} all-gather(bf16[1,1,256]{2,1,0:T(2,128)(2,1)S(1)} %reshape.985), channel_id=2, replica_groups=mesh['seq'=32,'tp'=4] {'seq'}, dimensions={0}, use_global_device_ids=true | all-gather | bytes 16896 | tf_op jit(solution)/shard_map/all_gather | solution.py:24
  73.3 28.3 %all-gather.5.cloned.1.call-done = bf16[32,256,512]{2,1,0:T(8,128)(2,1)} async-done(((bf16[1,256,512]{2,1,0:T(8,128)(2,1)}), bf16[32,256,512]{2,1,0:T(8,128)(2,1)}) %all-gather.5.cloned.1.call-update) | async-done | bytes 8388624 | tf_op jit(solution)/shard_map/all_gather | solution.py:24
  101.6 36.2 %while.44 = (s32[]{:T(128)}, f32[1,256,512]{2,1,0:T(8,128)S(1)}, s32[]{:T(128)}, bf16[32,1,256]{2,1,0:T(2,128)(2,1)S(1)}, bf16[32,1,256,512]{3,2,1,0:T(8,128)(2,1)}, /*index=5*/s32[]{:T(128)}, s32[]{:T(128)}) while((s32[]{:T(128)}, f32[1,256,512]{2,1,0:T(8,128)S(1)}, s32[]{:T(128)}, bf16[32,1,256]{2,1,0:T(2,128)(2,1)S(1)}, ...), condition=%wide.region_9.10_spmd.clone, body=%wide.region_8.9_spmd.clone.sunk | while | flops 655620 | bytes 1313385 | solution.py:41
  101.6 1.1 fusion.125
  102.7 1.1 fusion.125
  103.9 1.1 fusion.125
  105.0 1.1 fusion.125
  106.1 1.1 fusion.125
  107.3 1.1 fusion.125
  108.4 1.1 fusion.125
  109.5 1.1 fusion.125
  110.7 1.1 fusion.125
  111.8 1.1 fusion.125
  112.9 1.1 fusion.125
  114.0 1.1 fusion.125
  115.2 1.1 fusion.125
  116.3 1.1 fusion.125
  117.4 1.1 fusion.125
  118.6 1.1 fusion.125
  119.7 1.1 fusion.125
  120.8 1.1 fusion.125
  122.0 1.1 fusion.125
  123.1 1.1 fusion.125
  124.2 1.1 fusion.125
  125.4 1.1 fusion.125
  126.5 1.1 fusion.125
  127.6 1.1 fusion.125
  128.8 1.1 fusion.125
  129.9 1.1 fusion.125
  131.0 1.1 fusion.125
  132.2 1.1 fusion.125
  133.3 1.1 fusion.125
  134.4 1.1 fusion.125
  135.5 1.1 fusion.125
  136.7 1.1 fusion.125
  137.8 1.5 broadcast_in_dim.240
  139.3 54.6 %while.42 = (s32[]{:T(128)}, f32[1,256,512]{2,1,0:T(8,128)S(1)}, bf16[8,1,256,512]{3,2,0,1:T(8,128)(2,1)}, f32[4,64,1,512]{3,1,2,0:T(8,128)}, s32[4,64]{1,0:T(4,...) while((s32[]{:T(128)}, f32[1,256,512]{2,1,0:T(8,128)S(1)}, ...), condition=%wide.region_17.18_spmd, body=%wide.region_11.17_spmd.sunk | while | flops 268659424 | bytes 8804605 | solution.py:260
  145.0 5.8 %conditional.2 = (bf16[8,1,256,512]{3,2,0,1:T(8,128)(2,1)}) conditional(s32[]{:T(128)} %convert_element_type.388, bf16[8,1,256,512]{3,2,0,1:T(8,128)(2,1)} %get-tuple-element.722, (pred[8]{0:T(512)(128)(4,1)S(1)}, s32[8]{0:T(128)S(1)}, s32[64]{0:T(128)S(1)}, bf16[1,64,1,256]{3,2,1,0:T(2,128)(2,1)S(1)}, f32[64,1,256]{2,1,0:T(1,128)S(1)}, ...), branch_computations={%region_14.14_spmd, %region_15.15_spmd} | conditional | flops 139086368 | bytes 5199492 | solution.py:114
  147.1 3.7 %fusion = bf16[8,1,256,512]{3,2,0,1:T(8,128)(2,1)} fusion(bf16[8,1,256,512]{3,2,0,1:T(8,128)(2,1)} %get-tuple-element.210, f32[256,512]{1,0:T(8,128)S(1)} %bitcast.271, f32[8,256]{1,0:T(8,128)S(1)} %exp.116, pred[8]{0:T(512)(128)(4,1)S(1)} %broadcast_compare_fusion, pred[8]{0:T(512)(128)(4,1)S(1)} %get-tuple-element.202, f32[8,256]{1,0:T(8,128)S(1)} %gather_fusion.1, ...), kind=kOutput, calls=%fused_computation.7 | convolution fusion | flops 139067392 | bytes 4932112 | tf_op jit(solution)/shard_map/while/body/eval_jaxpr/cond/branch_1_fun/rjhc,jhv->rhcv/dot_general | solution.py:106
  150.9 2.0 multiply_reduce_fusion.4
  163.2 2.0 multiply_reduce_fusion.4
  175.4 2.0 multiply_reduce_fusion.4
  187.6 2.0 multiply_reduce_fusion.4
  193.9 1.2 multiply_reduce_fusion.2
  195.2 2.8 fusion.56
  198.0 1.7 convolution_convert_fusion
  199.8 1.5 convert_element_type.287
  201.5 1.7 gather_fusion.4
  203.2 1.7 gather_fusion.3
  204.9 1.7 gather_fusion.2
  206.8 16.3 %reduce-scatter.2.cloned.1.call-done = bf16[256,512]{1,0:T(8,128)(2,1)} async-done(((bf16[256,2048]{1,0:T(8,128)(2,1)}), bf16[256,512]{1,0:T(8,128)(2,1)}) %reduce-scatter.2.cloned.1.call-update) | async-done | bytes 262160 | tf_op jit(solution)/shard_map/reduce_scatter | solution.py:264
  223.1 1.2 add_convert_fusion
  225.0 127.1 %all-reduce = (bf16[8,3,1024]{2,0,1:T(8,128)(2,1)S(1)}, bf16[8,512]{1,0:T(8,128)(2,1)S(1)}) all-reduce(bf16[8,3,1024]{2,0,1:T(8,128)(2,1)S(1)} %pad_maximum_fusion.1, bf16[8,512]{1,0:T(8,128)(2,1)S(1)} %select_convert_fusion.2), channel_id=1, replica_groups=mesh['seq'=32,'tp'=4] {'seq'}, use_global_device_ids=true, to_apply=%region_21.22 | all-reduce | flops 28672 | bytes 114688 | tf_op jit(solution)/shard_map/psum | solution.py:284
  352.7 3.3 all-to-all-start
  356.1 4.3 %convert_element_type.304 = f32[8,1,256,512]{3,2,1,0:T(8,128)} convert(bf16[8,1,256,512]{3,2,1,0:T(8,128)(2,1)} %all-reduce.3.cloned.1.call-done) | non-fusion elementwise | flops 1048576 | bytes 6291456 | tf_op jit(solution)/shard_map/convert_element_type | solution.py:285
  (248 shorter events, 57.9 us)
Async XLA Ops:
  7.2 190.9 %copy-start = (bf16[512,2048]{1,0:T(8,128)(2,1)S(1)}, bf16[512,2048]{1,0:T(8,128)(2,1)}, u32[]{:S(2)}) copy-start(bf16[512,2048]{1,0:T(8,128)(2,1)} %param.31) | copy-start | bytes 6291460
  7.2 94.4 %all-gather.5.cloned.1.call-start = ((), (), s32[]{:S(2)}) async-start(), calls=%async_computation.4 | async-start | bytes 8650752 | tf_op jit(solution)/shard_map/all_gather | solution.py:24
  8.9 6.1 %copy-start.8 = (s32[8]{0:T(128)S(1)}, s32[8]{0:T(128)}, u32[]{:S(2)}) copy-start(s32[8]{0:T(128)} %param.34) | copy-start | bytes 100
  8.9 6.1 %copy-start.14 = (s32[8]{0:T(128)S(1)}, s32[8]{0:T(128)}, u32[]{:S(2)}) copy-start(s32[8]{0:T(128)} %param.35) | copy-start | bytes 100
  8.9 6.7 %copy-start.6 = (f32[4,1024]{1,0:T(4,128)S(1)}, f32[4,1024]{1,0:T(4,128)}, u32[]{:S(2)}) copy-start(f32[4,1024]{1,0:T(4,128)} %param.25) | copy-start | bytes 49156
  8.9 6.7 %copy-start.1 = (bf16[256,2048]{1,0:T(8,128)(2,1)S(1)}, bf16[256,2048]{1,0:T(8,128)(2,1)}, u32[]{:S(2)}) copy-start(bf16[256,2048]{1,0:T(8,128)(2,1)} %param.22) | copy-start | bytes 3145732
  8.9 6.7 %copy-start.9 = (bf16[2048,16]{0,1:T(8,128)(2,1)S(1)}, bf16[2048,16]{0,1:T(8,128)(2,1)}, u32[]{:S(2)}) copy-start(bf16[2048,16]{0,1:T(8,128)(2,1)} %param.26) | copy-start | bytes 196612
  8.9 6.7 %copy-start.11 = (f32[2048]{0:T(1024)S(1)}, f32[2048]{0:T(1024)}, u32[]{:S(2)}) copy-start(f32[2048]{0:T(1024)} %param.23) | copy-start | bytes 24580
  9.0 7.1 %copy-start.10 = (bf16[16,256]{1,0:T(8,128)(2,1)S(1)}, bf16[16,256]{1,0:T(8,128)(2,1)}, u32[]{:S(2)}) copy-start(bf16[16,256]{1,0:T(8,128)(2,1)} %param.27) | copy-start | bytes 24580
  9.0 7.1 %copy-start.13 = (f32[256]{0:T(256)S(1)}, f32[256]{0:T(256)}, u32[]{:S(2)}) copy-start(f32[256]{0:T(256)} %param.28) | copy-start | bytes 3076
  12.9 0.8 copy-start.4
  13.7 4.1 %collective-permute-start = (bf16[3,1024]{1,0:T(4,128)(2,1)S(1)}, bf16[3,1024]{1,0:T(4,128)(2,1)S(1)}, u32[]{:S(2)}, u32[]{:S(2)}) collective-permute-start(bf16[3,1024]{1,0:T(4,128)(2,1)S(1)} %slice.111), channel_id=1, source_target_pairs={{0,4},{4,8},{8,12},{12,16},{16,20},{20,24},{24,28},{28,32},{32,36}... | collective-permute-start | bytes 18440 | tf_op jit(solution)/shard_map/ppermute | solution.py:47
  44.3 178.8 %reduce-scatter.2.cloned.1.call-start = ((), (), s32[]{:S(2)}) async-start(), calls=%async_computation.2 | async-start | bytes 1310720 | tf_op jit(solution)/shard_map/reduce_scatter | solution.py:264
  139.3 55.9 %copy-start.12 = (f32[512]{0:T(512)S(1)}, f32[512]{0:T(512)}, u32[]{:S(2)}) copy-start(f32[512]{0:T(512)} %param.30) | copy-start | bytes 6148
  198.0 1.8 copy-start.2
  199.8 156.3 %all-reduce.3.cloned.1.call-start = ((), (), s32[]{:S(2)}) async-start(), calls=%async_computation.3 | async-start | bytes 4194304 | tf_op jit(solution)/shard_map/psum | solution.py:285
  224.3 128.4 %copy-start.5 = (bf16[256,512]{1,0:T(8,128)(2,1)}, bf16[256,512]{1,0:T(8,128)(2,1)S(1)}, u32[]{:S(2)}) copy-start(bf16[256,512]{1,0:T(8,128)(2,1)S(1)} %add_convert_fusion) | copy-start | bytes 786436
  352.7 8.9 %all-to-all-start = ((f32[4,8,512]{2,1,0:T(8,128)}), f32[4,8,512]{2,1,0:T(8,128)S(1)}, u32[]{:S(2)}, u32[]{:S(2)}) async-start(f32[4,8,512]{2,1,0:T(8,128)} %stack.6), calls=%async_computation.1 | async-start | bytes 131072 | tf_op jit(solution)/shard_map/all_to_all | solution.py:17
  356.0 6.2 %copy-start.3 = (bf16[250,2048]{1,0:T(8,128)(2,1)S(1)}, bf16[250,2048]{1,0:T(8,128)(2,1)}, u32[]{:S(2)}) copy-start(bf16[250,2048]{1,0:T(8,128)(2,1)} %param.33) | copy-start | bytes 3072004
  356.0 6.2 %copy-start.7 = (f32[2048]{0:T(1024)S(1)}, f32[2048]{0:T(1024)}, u32[]{:S(2)}) copy-start(f32[2048]{0:T(1024)} %param.32) | copy-start | bytes 24580
Sparse Core Ops, SparseCore 0:
  44.4 57.1 all-gather.4
  199.9 23.1 reduce-scatter.1
  227.0 107.2 all-reduce.2
